TPU v7x, 32 devices: a whole 2x2x4 slice. The times are simulated.
32 devices in a mesh: groups: 2 (over y), lat: 8 (over z, x), seed: 2 (over core).
Axes of the slice: x: 2, y: 2, z: 4, core: 2. Of those that a mesh axis runs over, the one named last changes fastest.
Arguments:
- activations: bfloat16 [512, 2048], P(('groups', 'seed'), 'lat'), parts along dimension 0, may hold values from -6 to 6
- bag_rows: int32 [4, 256], P(('groups', 'seed')), parts along dimension 0, may hold values from 0 to 255
- keep_cols: int32 [4, 2048], P(('groups', 'seed')), parts along dimension 0, may hold values 0 or 1
- enc_weight: bfloat16 [4, 16384, 2048], P(('groups', 'seed'), 'lat'), parts along dimension 0, may hold values from -0.125 to 0.125
- enc_bias: float32 [4, 16384], P(('groups', 'seed'), 'lat'), parts along dimension 0, may hold values from -3 to 3
- dec_weight: bfloat16 [4, 16384, 2048], P(('groups', 'seed'), 'lat'), parts along dimension 0, may hold values from -0.0625 to 0.0625
- dec_bias: float32 [4, 2048], P(('groups', 'seed')), parts along dimension 0, may hold values from -3 to 3
- first_moment: bfloat16 [4, 16384, 2048], P(('groups', 'seed'), 'lat'), parts along dimension 0, may hold values from -0.3125 to 0.3125
- second_moment: bfloat16 [4, 16384, 2048], P(('groups', 'seed'), 'lat'), parts along dimension 0, may hold values from 9.9658966e-05 to 0.0099487305
Outputs:
- new_weight: bfloat16 [4, 16384, 2048], P(('groups', 'seed'), 'lat'), parts along dimension 0
- new_first: bfloat16 [4, 16384, 2048], P(('groups', 'seed'), 'lat'), parts along dimension 0
- new_second: bfloat16 [4, 16384, 2048], P(('groups', 'seed'), 'lat'), parts along dimension 0
There are 2 independent parts, one for each index of `groups`. A program takes and returns all parts, laid end to end along the dimension named above; each array names one. Nothing has to cross between parts.
All inputs are finite; a program needn't handle non-finite values. No bound on the sum of `keep_cols` on one device may be relied on, other than what follows from the above.
Results may differ from a plain program's by a relative error of at most 0.012.
The roundings to bfloat16 on the way count: a program that leaves them out, or rounds other values in their place, can miss the bound.
Values may be sent and summed in bfloat16 or wider, within the bound.
No kernel may reach another device: no remote copies, remote signals or barrier semaphores. Data moves between devices by JAX's collectives and lax.ppermute only.
A program may use at most 128 MiB of HBM per device.

v0:
```python
import jax
import jax.numpy as jnp
from jax import lax
from jax.sharding import PartitionSpec as P

sparsity = 0.2
beta_one = 0.9
beta_two = 0.95
corr_one = 1.0 - 0.9**10
corr_two = 1.0 - 0.95**10
adam_eps = 1e-08
rate_step = 0.001
decay_rate = 0.1


def local(
    activations,
    bag_rows,
    keep_cols,
    enc_weight,
    enc_bias,
    dec_weight,
    dec_bias,
    first_moment,
    second_moment,
):
    half_rows = lax.all_gather(activations, "lat", axis=1, tiled=True)
    gathered = lax.all_gather(half_rows, "seed", axis=0, tiled=True)
    row_order = bag_rows[0]
    sample = jnp.take(gathered, row_order, axis=0)
    weight_in = enc_weight[0]
    decoder = dec_weight[0]
    bias_dec = dec_bias[0]
    keep = keep_cols[0].astype(jnp.float32)
    centered = (sample.astype(jnp.float32) - bias_dec).astype(jnp.bfloat16)
    pre_t = lax.dot_general(
        weight_in, centered, (((1,), (1,)), ((), ())), preferred_element_type=jnp.float32
    )
    pre_t = pre_t + enc_bias[0][:, None]
    latent_t = jnp.maximum(pre_t, 0.0).astype(jnp.bfloat16)
    partial_sum = lax.dot_general(
        latent_t, decoder, (((0,), (0,)), ((), ())), preferred_element_type=jnp.float32
    )
    total = lax.psum(partial_sum, "lat")
    error = ((total + bias_dec - sample.astype(jnp.float32)) * keep).astype(jnp.bfloat16)
    back_t = lax.dot_general(
        decoder, error, (((1,), (1,)), ((), ())), preferred_element_type=jnp.float32
    )
    row_norm = jnp.sqrt(jnp.sum(jnp.square(decoder.astype(jnp.float32)), axis=1) + 1e-06)
    token_total = sample.shape[0]
    d_pre_t = (
        jnp.where(pre_t > 0, 2.0 * back_t + sparsity * row_norm[:, None], 0.0) / token_total
    ).astype(jnp.bfloat16)
    grad = jnp.dot(d_pre_t, centered, preferred_element_type=jnp.float32)
    moment_one = beta_one * first_moment[0].astype(jnp.float32) + (1.0 - beta_one) * grad
    moment_two = beta_two * second_moment[0].astype(jnp.float32) + (1.0 - beta_two) * grad * grad
    direction = moment_one / corr_one / (jnp.sqrt(moment_two / corr_two) + adam_eps)
    old = weight_in.astype(jnp.float32)
    updated = (old - rate_step * (direction + decay_rate * old)).astype(jnp.bfloat16)
    return (
        updated[None],
        moment_one.astype(jnp.bfloat16)[None],
        moment_two.astype(jnp.bfloat16)[None],
    )


def solution(mesh):
    return jax.shard_map(
        local,
        mesh=mesh,
        in_specs=(
            P(("groups", "seed"), "lat"),
            P(("groups", "seed"), None),
            P(("groups", "seed"), None),
            P(("groups", "seed"), "lat", None),
            P(("groups", "seed"), "lat"),
            P(("groups", "seed"), "lat", None),
            P(("groups", "seed"), None),
            P(("groups", "seed"), "lat", None),
            P(("groups", "seed"), "lat", None),
        ),
        out_specs=(
            P(("groups", "seed"), "lat", None),
            P(("groups", "seed"), "lat", None),
            P(("groups", "seed"), "lat", None),
        ),
        check_vma=False,
    )
```

profile of v0, /device:TPU:0, one launch (start us, length us, event | category | flops | bytes accessed | tf_op | source)
XLA Modules:
  0.0 222.0 jit_solution(16715430085450274316)
XLA Ops:
  7.2 0.0 copy-start
  7.2 0.0 copy-start.2
  7.2 0.0 all-gather.2.cloned.1.call-start
  7.2 35.4 %all_gather.6 = bf16[128,2048]{1,0:T(8,128)(2,1)} all-gather(bf16[128,256]{1,0:T(8,128)(2,1)} %param.9), channel_id=1, replica_groups=mesh['groups'=2,'lat'=8,'seed'=2] {'lat'}, dimensions={1}, use_global_device_ids=true | all-gather | bytes 589824 | tf_op jit(solution)/shard_map/all_gather | solution.py:27
  42.6 0.0 all-gather.2.cloned.1.call-update
  42.7 0.0 all-reduce.2.cloned.1.call-start
  42.7 0.7 compare_select_fusion
  43.4 0.7 compare_and_fusion
  44.1 8.8 %all-gather.2.cloned.1.call-done = bf16[256,2048]{1,0:T(8,128)(2,1)} async-done(((bf16[128,2048]{1,0:T(8,128)(2,1)}), bf16[256,2048]{1,0:T(8,128)(2,1)}) %all-gather.2.cloned.1.call-update) | async-done | bytes 1048592 | tf_op jit(solution)/shard_map/all_gather | solution.py:28
  52.9 3.7 %gather_fusion = bf16[256,2048]{1,0:T(8,128)(2,1)S(1)} fusion(bf16[256,2048]{1,0:T(8,128)(2,1)} %all-gather.2.cloned.1.call-done, s32[1024]{0:T(1024)S(1)} %pad_clamp_fusion), kind=kCustom, calls=%fused_computation | custom fusion | bytes 2098176 | tf_op jit(solution)/shard_map/jit(_take)/gather | solution.py:30
  56.6 0.0 copy-done
  56.6 0.0 copy-done.2
  56.7 5.8 %fusion.27 = f32[256,2048]{1,0:T(8,128)S(1)} fusion(bf16[1,2048,2048]{2,1,0:T(8,128)(2,1)} %param.12, f32[2048]{0:T(1024)S(1)} %bitcast.64, f32[2048]{0:T(1024)S(1)} %bitcast.59, bf16[256,2048]{1,0:T(8,128)(2,1)S(1)} %gather_fusion, pred[256]{0:T(512)(128)(4,1)S(1)} %compare_and_fusion), kind=kOutput, calls=%fused_computation.27 | convolution fusion | flops 2150105088 | bytes 11550976 | tf_op jit(solution)/shard_map/dot_general | solution.py:36
  62.4 0.0 copy-start.1
  62.5 7.0 %fusion.10 = f32[256,2048]{1,0:T(8,128)} fusion(bf16[1,2048,2048]{2,1,0:T(8,128)(2,1)} %param.14, f32[256,2048]{1,0:T(8,128)S(1)} %fusion.27), kind=kOutput, calls=%fused_computation.16 | convolution fusion | flops 2148532224 | bytes 12582912 | tf_op jit(solution)/shard_map/dot_general | solution.py:41
  69.5 0.0 all-reduce.2.cloned.1.call-update
  69.5 0.0 copy-done.1
  69.5 5.1 %multiply_reduce_fusion = f32[2048]{0:T(1024)S(1)} fusion(bf16[1,2048,2048]{2,1,0:T(8,128)(2,1)} %param.14), kind=kLoop, calls=%fused_computation.9 | loop fusion | flops 12580864 | bytes 8396800 | tf_op jit(solution)/shard_map/reduce_sum | solution.py:49
  74.6 98.0 %all-reduce.2.cloned.1.call-done = f32[256,2048]{1,0:T(8,128)} async-done(((f32[256,2048]{1,0:T(8,128)}), f32[256,2048]{1,0:T(8,128)}) %all-reduce.2.cloned.1.call-update) | async-done | bytes 2097168 | tf_op jit(solution)/shard_map/psum | solution.py:44
  172.7 14.7 %fusion.34 = f32[2048,2048]{1,0:T(8,128)} fusion(bf16[1,2048,2048]{2,1,0:T(8,128)(2,1)} %param.14, f32[256,2048]{1,0:T(8,128)S(1)} %fusion.27, f32[256,2048]{1,0:T(8,128)} %all-reduce.2.cloned.1.call-done, f32[2048]{0:T(1024)S(1)} %sqrt_multiply_fusion, f32[2048]{0:T(1024)S(1)} %bitcast.61, f32[2048]{0:T(1024)S(1)} %bitcast.60, ...), kind=kOutput, calls=%fused_computation.29 | convolution fusion | flops 4303355904 | bytes 30433536 | tf_op jit(solution)/shard_map/dot_general | solution.py:54
  187.3 27.9 %fusion.6 = (bf16[1,2048,2048]{2,1,0:T(8,128)(2,1)}, bf16[1,2048,2048]{2,1,0:T(8,128)(2,1)}, bf16[1,2048,2048]{2,1,0:T(8,128)(2,1)}) fusion(f32[2048,2048]{1,0:T(8,128)} %fusion.34, bf16[1,2048,2048]{2,1,0:T(8,128)(2,1)} %param.17, bf16[1,2048,2048]{2,1,0:T(8,128)(2,1)} %param.16, bf16[1,2048,2048]{2,1,0:T(8,128)(2,1)} %param.12), kind=kLoop, calls=%fused_computation.12 | loop fusion | flops 88080384 | bytes 67108864 | tf_op jit(solution)/shard_map/broadcast_in_dim | solution.py:63
  (3 shorter events, 0.0 us)
Async XLA Ops:
  7.2 49.5 %copy-start = (f32[1,2048]{1,0:T(1,128)S(1)}, f32[1,2048]{1,0:T(1,128)}, u32[]{:S(2)}) copy-start(f32[1,2048]{1,0:T(1,128)} %param.15) | copy-start | bytes 24580
  7.2 49.5 %copy-start.2 = (f32[1,2048]{1,0:T(1,128)S(1)}, f32[1,2048]{1,0:T(1,128)}, u32[]{:S(2)}) copy-start(f32[1,2048]{1,0:T(1,128)} %param.13) | copy-start | bytes 24580
  7.2 45.7 %all-gather.2.cloned.1.call-start = ((), (), s32[]{:S(2)}) async-start(), calls=%async_computation | async-start | bytes 1572864 | tf_op jit(solution)/shard_map/all_gather | solution.py:28
  42.7 130.0 %all-reduce.2.cloned.1.call-start = ((), (), s32[]{:S(2)}) async-start(), calls=%async_computation.1 | async-start | bytes 4194304 | tf_op jit(solution)/shard_map/psum | solution.py:44
  62.4 7.1 %copy-start.1 = (s32[1,2048]{1,0:T(1,128)S(1)}, s32[1,2048]{1,0:T(1,128)}, u32[]{:S(2)}) copy-start(s32[1,2048]{1,0:T(1,128)} %param.11) | copy-start | bytes 24580
Sparse Core Ops, SparseCore 0:
  42.8 10.0 all-gather.1
  69.6 103.0 all-reduce.1
where the time goes:
time: 222 us
  waiting for transfers between devices  107 us (48%)
  blocking collectives  35.4 us (16%)
  other arithmetic  34.3 us (15%)
  matrix products  27.5 us (12%)
  between operations  14.1 us (6%)
  local copies, waits for them, and re-layouts  3.74 us (2%)
    psum x1, waiting for transfers between devices, local(): total = lax.psum(partial_sum, 'lat')  98 us
    all_gather x1, blocking collectives, local(): half_rows = lax.all_gather(activations, 'lat', axis=1, tiled=True)  35.4 us
    broadcast_in_dim x1, other arithmetic, local(): moment_two.astype(jnp.bfloat16)[None]  27.9 us
    dot_general x1, matrix products, local(): grad = jnp.dot(d_pre_t, centered, preferred_element_type=jnp.float32)  14.7 us
    all_gather x1, waiting for transfers between devices, local(): gathered = lax.all_gather(half_rows, 'seed', axis=0, tiled=True)  8.8 us
    dot_general x1, matrix products, local(): lax.dot_general(latent_t, decoder, (((0,), (0,)), ((), ())), preferred_el...  7.04 us
    dot_general x1, matrix products, local(): lax.dot_general(weight_in, centered, (((1,), (1,)), ((), ())), preferred_...  5.77 us
    reduce_sum x1, other arithmetic, local(): jnp.sum(jnp.square(decoder.astype(jnp.float32)), axis=1) + 1e-06  5.08 us
  transfers between devices with their start and end apart: 2, of which 2 were waited for; matrix products, arithmetic and copies ran while one was open for 3% of the time, Pallas kernels for 0%

commit v1 on v0

--- a/solution.py
+++ b/solution.py
@@ -13,6 +13,24 @@
 decay_rate = 0.1
 
 
+def in_order(blocks, dim):
+    shape = list(blocks.shape[1:])
+    shape[dim] *= blocks.shape[0]
+    return jnp.moveaxis(blocks, 0, dim).reshape(shape)
+
+
+def grow_blocks(x, axis):
+    size = lax.axis_size(axis)
+    blocks = x[None]
+    for level in range(size.bit_length() - 1):
+        apart = 1 << level
+        partner_block = lax.ppermute(blocks, axis, [(i, i ^ apart) for i in range(size)])
+        both = jnp.stack([blocks, partner_block])
+        upper = lax.axis_index(axis) >> level & 1
+        blocks = jnp.where(upper == 0, both, both[::-1]).reshape(-1, *x.shape)
+    return blocks
+
+
 def local(
     activations,
     bag_rows,
@@ -24,7 +42,7 @@
     first_moment,
     second_moment,
 ):
-    half_rows = lax.all_gather(activations, "lat", axis=1, tiled=True)
+    half_rows = in_order(grow_blocks(activations, "lat"), 1)
     gathered = lax.all_gather(half_rows, "seed", axis=0, tiled=True)
     row_order = bag_rows[0]
     sample = jnp.take(gathered, row_order, axis=0)

time: 222 us -> 212 us (0.955)
  blocking collectives: 35.4 us -> 0 us
  waiting for transfers between devices: 107 us -> 122 us
  starting transfers between devices: 0.08 us -> 8.35 us
    all_gather x1 -> x0, blocking collectives: 35.4 us -> none  [local(): half_rows = lax.all_gather(activations, 'lat', axis=1, tiled=True)]
    ppermute x0 -> x3, waiting for transfers between devices: none -> 15 us  [grow_blocks(): lax.ppermute(blocks, axis, [(i, i ^ apart) for i in range(size)])]
    ppermute x0 -> x3, starting transfers between devices: none -> 8.27 us  [grow_blocks(): lax.ppermute(blocks, axis, [(i, i ^ apart) for i in range(size)])]
  transfers between devices with their start and end apart: 2 -> 5, of which waited for: 2 -> 5; matrix products, arithmetic and copies ran while one was open for 3% -> 3% of each run, Pallas kernels for 0% -> 0%
where the time goes in v1:
time: 212 us
  waiting for transfers between devices  122 us (58%)
  other arithmetic  35.4 us (17%)
  matrix products  27.5 us (13%)
  between operations  14.1 us (7%)
  starting transfers between devices  8.35 us (4%)
  local copies, waits for them, and re-layouts  4.58 us (2%)
    psum x1, waiting for transfers between devices, local(): total = lax.psum(partial_sum, 'lat')  97.9 us
    broadcast_in_dim x1, other arithmetic, local(): moment_two.astype(jnp.bfloat16)[None]  27.9 us
    ppermute x3, waiting for transfers between devices, grow_blocks(): lax.ppermute(blocks, axis, [(i, i ^ apart) for i in range(size)])  15 us
    dot_general x1, matrix products, local(): grad = jnp.dot(d_pre_t, centered, preferred_element_type=jnp.float32)  14.7 us
    all_gather x1, waiting for transfers between devices, local(): gathered = lax.all_gather(half_rows, 'seed', axis=0, tiled=True)  8.95 us
    ppermute x3, starting transfers between devices, grow_blocks(): lax.ppermute(blocks, axis, [(i, i ^ apart) for i in range(size)])  8.27 us
    dot_general x1, matrix products, local(): lax.dot_general(latent_t, decoder, (((0,), (0,)), ((), ())), preferred_el...  7.04 us
    dot_general x1, matrix products, local(): lax.dot_general(weight_in, centered, (((1,), (1,)), ((), ())), preferred_...  5.77 us
  transfers between devices with their start and end apart: 5, of which 5 were waited for; matrix products, arithmetic and copies ran while one was open for 3% of the time, Pallas kernels for 0%

profile of v1, /device:TPU:0, one launch (start us, length us, event | category | flops | bytes accessed | tf_op | source)
XLA Modules:
  0.0 212.0 jit_solution(11551554040054196578)
XLA Ops:
  7.2 0.0 copy-start
  7.2 0.0 copy-start.2
  7.2 0.0 all-gather.2.cloned.1.call-start
  7.2 3.0 %collective-permute-start = (bf16[1,128,256]{2,1,0:T(8,128)(2,1)}, bf16[1,128,256]{2,1,0:T(8,128)(2,1)S(1)}, u32[]{:S(2)}, u32[]{:S(2)}) collective-permute-start(bf16[1,128,256]{2,1,0:T(8,128)(2,1)} %bitcast.85), channel_id=1, source_target_pairs={{0,2},{2,0},{4,6},{6,4},{8,10},{10,8},{12,14},{14,12},{1,3},{3,1},... | collective-permute-start | bytes 196616 | tf_op jit(solution)/shard_map/ppermute | solution.py:27
  10.2 2.5 %collective-permute-done = bf16[1,128,256]{2,1,0:T(8,128)(2,1)S(1)} collective-permute-done((bf16[1,128,256]{2,1,0:T(8,128)(2,1)}, bf16[1,128,256]{2,1,0:T(8,128)(2,1)S(1)}, u32[]{:S(2)}, u32[]{:S(2)}) %collective-permute-start) | collective-permute-done | bytes 65568 | tf_op jit(solution)/shard_map/ppermute | solution.py:27
  12.7 0.9 pad_maximum_fusion.2
  13.6 2.2 %collective-permute-start.1 = (bf16[2,128,256]{2,1,0:T(8,128)(2,1)S(1)}, bf16[2,128,256]{2,1,0:T(8,128)(2,1)S(1)}, u32[]{:S(2)}, u32[]{:S(2)}) collective-permute-start(bf16[2,128,256]{2,1,0:T(8,128)(2,1)S(1)} %get-tuple-element.7), channel_id=1, source_target_pairs={{0,4},{2,6},{4,0},{6,2},{8,12},{10,14},{12,8},{14,10},{1,5},{3,7},... | collective-permute-start | bytes 393224 | tf_op jit(solution)/shard_map/ppermute | solution.py:27
  15.8 2.9 %collective-permute-done.1 = bf16[2,128,256]{2,1,0:T(8,128)(2,1)S(1)} collective-permute-done((bf16[2,128,256]{2,1,0:T(8,128)(2,1)S(1)}, bf16[2,128,256]{2,1,0:T(8,128)(2,1)S(1)}, u32[]{:S(2)}, u32[]{:S(2)}) %collective-permute-start.1) | collective-permute-done | bytes 131104 | tf_op jit(solution)/shard_map/ppermute | solution.py:27
  18.7 0.1 reverse_select_fusion.1
  18.8 3.1 %collective-permute-start.2 = (bf16[4,128,256]{2,1,0:T(8,128)(2,1)S(1)}, bf16[4,128,256]{2,1,0:T(8,128)(2,1)S(1)}, u32[]{:S(2)}, u32[]{:S(2)}) collective-permute-start(bf16[4,128,256]{2,1,0:T(8,128)(2,1)S(1)} %bitcast.78), channel_id=1, source_target_pairs={{0,8},{2,10},{4,12},{6,14},{8,0},{10,2},{12,4},{14,6},{1,9},{3,11}... | collective-permute-start | bytes 786440 | tf_op jit(solution)/shard_map/ppermute | solution.py:27
  21.9 9.6 %collective-permute-done.2 = bf16[4,128,256]{2,1,0:T(8,128)(2,1)S(1)} collective-permute-done((bf16[4,128,256]{2,1,0:T(8,128)(2,1)S(1)}, bf16[4,128,256]{2,1,0:T(8,128)(2,1)S(1)}, u32[]{:S(2)}, u32[]{:S(2)}) %collective-permute-start.2) | collective-permute-done | bytes 262176 | tf_op jit(solution)/shard_map/ppermute | solution.py:27
  31.5 0.1 pad_maximum_fusion
  31.6 0.1 reverse_select_fusion
  31.7 0.8 copy.15
  32.5 0.0 all-gather.2.cloned.1.call-update
  32.5 0.0 all-reduce.2.cloned.1.call-start
  32.6 0.7 compare_select_fusion
  33.3 0.7 compare_and_fusion
  34.0 9.0 %all-gather.2.cloned.1.call-done = bf16[256,2048]{1,0:T(8,128)(2,1)} async-done(((bf16[128,2048]{1,0:T(8,128)(2,1)}), bf16[256,2048]{1,0:T(8,128)(2,1)}) %all-gather.2.cloned.1.call-update) | async-done | bytes 1048592 | tf_op jit(solution)/shard_map/all_gather | solution.py:46
  42.9 3.7 %gather_fusion = bf16[256,2048]{1,0:T(8,128)(2,1)S(1)} fusion(bf16[256,2048]{1,0:T(8,128)(2,1)} %all-gather.2.cloned.1.call-done, s32[1024]{0:T(1024)S(1)} %pad_clamp_fusion), kind=kCustom, calls=%fused_computation | custom fusion | bytes 2098176 | tf_op jit(solution)/shard_map/jit(_take)/gather | solution.py:48
  46.7 0.0 copy-done
  46.7 0.0 copy-done.2
  46.7 5.8 %fusion.27 = f32[256,2048]{1,0:T(8,128)S(1)} fusion(bf16[1,2048,2048]{2,1,0:T(8,128)(2,1)} %param.12, f32[2048]{0:T(1024)S(1)} %bitcast.90, f32[2048]{0:T(1024)S(1)} %bitcast.82, bf16[256,2048]{1,0:T(8,128)(2,1)S(1)} %gather_fusion, pred[256]{0:T(512)(128)(4,1)S(1)} %compare_and_fusion), kind=kOutput, calls=%fused_computation.27 | convolution fusion | flops 2150105088 | bytes 11550976 | tf_op jit(solution)/shard_map/dot_general | solution.py:54
  52.5 0.0 copy-start.1
  52.5 7.0 %fusion.10 = f32[256,2048]{1,0:T(8,128)} fusion(bf16[1,2048,2048]{2,1,0:T(8,128)(2,1)} %param.14, f32[256,2048]{1,0:T(8,128)S(1)} %fusion.27), kind=kOutput, calls=%fused_computation.16 | convolution fusion | flops 2148532224 | bytes 12582912 | tf_op jit(solution)/shard_map/dot_general | solution.py:59
  59.5 0.0 all-reduce.2.cloned.1.call-update
  59.5 0.0 copy-done.1
  59.6 5.1 %multiply_reduce_fusion = f32[2048]{0:T(1024)S(1)} fusion(bf16[1,2048,2048]{2,1,0:T(8,128)(2,1)} %param.14), kind=kLoop, calls=%fused_computation.9 | loop fusion | flops 12580864 | bytes 8396800 | tf_op jit(solution)/shard_map/reduce_sum | solution.py:67
  64.7 97.9 %all-reduce.2.cloned.1.call-done = f32[256,2048]{1,0:T(8,128)} async-done(((f32[256,2048]{1,0:T(8,128)}), f32[256,2048]{1,0:T(8,128)}) %all-reduce.2.cloned.1.call-update) | async-done | bytes 2097168 | tf_op jit(solution)/shard_map/psum | solution.py:62
  162.6 14.7 %fusion.34 = f32[2048,2048]{1,0:T(8,128)} fusion(bf16[1,2048,2048]{2,1,0:T(8,128)(2,1)} %param.14, f32[256,2048]{1,0:T(8,128)S(1)} %fusion.27, f32[256,2048]{1,0:T(8,128)} %all-reduce.2.cloned.1.call-done, f32[2048]{0:T(1024)S(1)} %sqrt_multiply_fusion, f32[2048]{0:T(1024)S(1)} %bitcast.84, f32[2048]{0:T(1024)S(1)} %bitcast.83, ...), kind=kOutput, calls=%fused_computation.29 | convolution fusion | flops 4303355904 | bytes 30433536 | tf_op jit(solution)/shard_map/dot_general | solution.py:72
  177.3 27.9 %fusion.6 = (bf16[1,2048,2048]{2,1,0:T(8,128)(2,1)}, bf16[1,2048,2048]{2,1,0:T(8,128)(2,1)}, bf16[1,2048,2048]{2,1,0:T(8,128)(2,1)}) fusion(f32[2048,2048]{1,0:T(8,128)} %fusion.34, bf16[1,2048,2048]{2,1,0:T(8,128)(2,1)} %param.17, bf16[1,2048,2048]{2,1,0:T(8,128)(2,1)} %param.16, bf16[1,2048,2048]{2,1,0:T(8,128)(2,1)} %param.12), kind=kLoop, calls=%fused_computation.12 | loop fusion | flops 88080384 | bytes 67108864 | tf_op jit(solution)/shard_map/broadcast_in_dim | solution.py:81
  (5 shorter events, 0.1 us)
Async XLA Ops:
  7.2 39.5 %copy-start = (f32[1,2048]{1,0:T(1,128)S(1)}, f32[1,2048]{1,0:T(1,128)}, u32[]{:S(2)}) copy-start(f32[1,2048]{1,0:T(1,128)} %param.15) | copy-start | bytes 24580
  7.2 39.5 %copy-start.2 = (f32[1,2048]{1,0:T(1,128)S(1)}, f32[1,2048]{1,0:T(1,128)}, u32[]{:S(2)}) copy-start(f32[1,2048]{1,0:T(1,128)} %param.13) | copy-start | bytes 24580
  7.2 35.7 %all-gather.2.cloned.1.call-start = ((), (), s32[]{:S(2)}) async-start(), calls=%async_computation | async-start | bytes 1572864 | tf_op jit(solution)/shard_map/all_gather | solution.py:46
  7.2 5.5 %collective-permute-start = (bf16[1,128,256]{2,1,0:T(8,128)(2,1)}, bf16[1,128,256]{2,1,0:T(8,128)(2,1)S(1)}, u32[]{:S(2)}, u32[]{:S(2)}) collective-permute-start(bf16[1,128,256]{2,1,0:T(8,128)(2,1)} %bitcast.85), channel_id=1, source_target_pairs={{0,2},{2,0},{4,6},{6,4},{8,10},{10,8},{12,14},{14,12},{1,3},{3,1},... | collective-permute-start | bytes 196616 | tf_op jit(solution)/shard_map/ppermute | solution.py:27
  13.6 5.1 %collective-permute-start.1 = (bf16[2,128,256]{2,1,0:T(8,128)(2,1)S(1)}, bf16[2,128,256]{2,1,0:T(8,128)(2,1)S(1)}, u32[]{:S(2)}, u32[]{:S(2)}) collective-permute-start(bf16[2,128,256]{2,1,0:T(8,128)(2,1)S(1)} %get-tuple-element.7), channel_id=1, source_target_pairs={{0,4},{2,6},{4,0},{6,2},{8,12},{10,14},{12,8},{14,10},{1,5},{3,7},... | collective-permute-start | bytes 393224 | tf_op jit(solution)/shard_map/ppermute | solution.py:27
  18.8 12.7 %collective-permute-start.2 = (bf16[4,128,256]{2,1,0:T(8,128)(2,1)S(1)}, bf16[4,128,256]{2,1,0:T(8,128)(2,1)S(1)}, u32[]{:S(2)}, u32[]{:S(2)}) collective-permute-start(bf16[4,128,256]{2,1,0:T(8,128)(2,1)S(1)} %bitcast.78), channel_id=1, source_target_pairs={{0,8},{2,10},{4,12},{6,14},{8,0},{10,2},{12,4},{14,6},{1,9},{3,11}... | collective-permute-start | bytes 786440 | tf_op jit(solution)/shard_map/ppermute | solution.py:27
  32.5 130.0 %all-reduce.2.cloned.1.call-start = ((), (), s32[]{:S(2)}) async-start(), calls=%async_computation.1 | async-start | bytes 4194304 | tf_op jit(solution)/shard_map/psum | solution.py:62
  52.5 7.1 %copy-start.1 = (s32[1,2048]{1,0:T(1,128)S(1)}, s32[1,2048]{1,0:T(1,128)}, u32[]{:S(2)}) copy-start(s32[1,2048]{1,0:T(1,128)} %param.11) | copy-start | bytes 24580
Sparse Core Ops, SparseCore 0:
  32.7 10.2 all-gather.1
  59.6 102.8 all-reduce.1
